TPU v7x, 128 devices: a whole 4x4x4 slice. The times are simulated.
128 devices in a mesh: seq: 32 (over z, x, y_lo), type: 4 (over y_hi, core).
Axes of the slice: x: 4, y: 4 (y_hi: 2, y_lo: 2; y = y_hi * 2 + y_lo), z: 4, core: 2. Of those that a mesh axis runs over, the one named last changes fastest.
Arguments:
- tokens: bfloat16 [17408, 1024], P(('seq', 'type')), may hold values from -60 to 60
- shift_scale: float32 [2, 1024], replicated, may hold values from -0.8 to 0.8
- branch_gate: float32 [1024], replicated, may hold values from 0.25 to 1.75
- final_gain: float32 [1024], replicated, may hold values from 0.5 to 1.5
- w_qkv: bfloat16 [3, 1024, 1024], P(None, None, 'type'), may hold values from -1 to 1
- w_out: bfloat16 [1024, 1024], P('type'), may hold values from -0.375 to 0.375
- type_ids: int32 [17408, 1], P(('seq', 'type')), may hold values from 0 to 7; in each aligned block of 136 rows (0 to 135, 136 to 271, ...) at most 51 rows name the same one
- head_w1: bfloat16 [8, 1024, 1024], P('type'), may hold values from -0.1875 to 0.1875
- head_b1: bfloat16 [8, 1024], P('type'), may hold values from -3 to 3
- head_w2: bfloat16 [8, 1024, 16], P('type'), may hold values from -0.1875 to 0.1875
Outputs:
- updated: bfloat16 [17408, 1024], P(('seq', 'type'))
- head_out: float32 [17408, 16], P(('seq', 'type'))
Inputs may be any that keep to these rules, and one draw needn't show every extreme that they name: `type_ids`: among the 136 tokens of one device no type occurs more than 51 times; some type occurs exactly 51 times on some devices.
All inputs are finite; a program needn't handle non-finite values.
Results may differ from a plain program's by a relative error of at most 0.014.
Values may be sent and summed in bfloat16 or wider, within the bound.
No kernel may reach another device: no remote copies, remote signals or barrier semaphores. Data moves between devices by JAX's collectives and lax.ppermute only.
A program may use at most 192 MiB of HBM per device.

v0:
```python
import jax
import jax.numpy as jnp
from jax import lax
from jax.sharding import PartitionSpec as P

HD = 64


def rms_normalize(values):
    squares = jnp.mean(values * values, axis=-1, keepdims=True)
    return values * lax.rsqrt(squares + 1e-06)


def absorb_block(state, query_heads, key_heads, value_heads):
    largest, totals, numer = state
    scores = jnp.einsum(
        "qhd,khd->hqk", query_heads, key_heads, preferred_element_type=jnp.float32
    ) * HD ** (-0.5)
    newmax = jnp.maximum(largest, jnp.max(scores, axis=-1))
    decay = jnp.exp(largest - newmax)
    weights = jnp.exp(scores - newmax[:, :, None])
    totals = totals * decay + jnp.sum(weights, axis=-1)
    update = jnp.einsum(
        "hqk,khd->qhd",
        weights.astype(jnp.bfloat16),
        value_heads,
        preferred_element_type=jnp.float32,
    )
    numer = numer * jnp.transpose(decay)[:, :, None] + update
    return (newmax, totals, numer)


def apply_heads(feature_slots, first_w, first_b, second_w):
    hidden = jnp.einsum(
        "...tcd,tdh->...tch", feature_slots, first_w, preferred_element_type=jnp.float32
    )
    hidden = jax.nn.gelu(hidden + first_b.astype(jnp.float32)[:, None, :]).astype(jnp.bfloat16)
    return jnp.einsum("...tch,tho->...tco", hidden, second_w, preferred_element_type=jnp.float32)


def body(
    tokens, shift_scale, branch_gate, final_gain, w_qkv, w_out, type_ids, head_w1, head_b1, head_w2
):
    inputs = tokens.astype(jnp.float32)
    modulated = (rms_normalize(inputs) * (1.0 + shift_scale[1]) + shift_scale[0]).astype(
        jnp.bfloat16
    )
    projected = jnp.einsum(
        "rd,ide->ire",
        lax.all_gather(modulated, "type", axis=0, tiled=True),
        w_qkv,
        preferred_element_type=jnp.float32,
    ).astype(jnp.bfloat16)
    queries = projected[0]
    local_keys = projected[1]
    local_values = projected[2]
    query_count = queries.shape[0]
    width = queries.shape[1]
    local_heads = width // HD
    query_heads = queries.reshape(query_count, local_heads, HD)
    initial = (
        jnp.full((local_heads, query_count), -1e30, jnp.float32),
        jnp.zeros((local_heads, query_count), jnp.float32),
        jnp.zeros((query_count, local_heads, HD), jnp.float32),
    )
    running = initial
    key_part = lax.all_gather(local_keys, "seq", axis=0, tiled=True)
    value_part = lax.all_gather(local_values, "seq", axis=0, tiled=True)
    row_total = key_part.shape[0]
    key_blocks = key_part.reshape(row_total // 512, 512, local_heads, HD)
    value_blocks = value_part.reshape(row_total // 512, 512, local_heads, HD)

    def advance(state, pair):
        return (absorb_block(state, query_heads, pair[0], pair[1]), None)

    running, unused = lax.scan(advance, running, (key_blocks, value_blocks))
    largest, totals, numer = running
    attended = (
        (numer / jnp.transpose(totals)[:, :, None]).astype(jnp.bfloat16).reshape(query_count, width)
    )
    mixed = lax.psum_scatter(
        jnp.dot(attended, w_out, preferred_element_type=jnp.float32),
        "type",
        scatter_dimension=0,
        tiled=True,
    )
    updated = (inputs + branch_gate * mixed).astype(jnp.bfloat16)
    final = (rms_normalize(updated.astype(jnp.float32)) * final_gain).astype(jnp.bfloat16)
    owned = head_w1.shape[0]
    owners = lax.axis_size("type")
    kinds_all = owned * owners
    capacity = 3 * tokens.shape[0] // 8
    kinds = type_ids[:, 0]
    onehot = (kinds[:, None] == jnp.arange(kinds_all, dtype=jnp.int32)[None, :]).astype(jnp.int32)
    ranks = jnp.sum((jnp.cumsum(onehot, axis=0) - onehot) * onehot, axis=1)
    slots = kinds * capacity + ranks
    slot_ids = jnp.arange(kinds_all * capacity, dtype=jnp.int32)
    dispatch = (slot_ids[:, None] == slots[None, :]).astype(jnp.bfloat16)
    packed = jnp.dot(dispatch, final, preferred_element_type=jnp.float32).astype(jnp.bfloat16)
    packed = packed.reshape(kinds_all, capacity, final.shape[1])
    first_w, first_b, second_w = (
        lax.all_gather(head_w1, "type", axis=0, tiled=True),
        lax.all_gather(head_b1, "type", axis=0, tiled=True),
        lax.all_gather(head_w2, "type", axis=0, tiled=True),
    )
    answers = apply_heads(packed, first_w, first_b, second_w)
    answers = answers.reshape(kinds_all * capacity, head_w2.shape[2])
    gather_back = (slots[:, None] == slot_ids[None, :]).astype(jnp.float32)
    head_out = jnp.dot(
        gather_back, answers, precision=lax.Precision.HIGHEST, preferred_element_type=jnp.float32
    )
    return (updated, head_out)


def solution(mesh):
    in_specs = (
        P(("seq", "type"), None),
        P(),
        P(),
        P(),
        P(None, None, "type"),
        P("type", None),
        P(("seq", "type"), None),
        P("type", None, None),
        P("type", None),
        P("type", None, None),
    )
    out_specs = (P(("seq", "type"), None), P(("seq", "type"), None))
    return jax.shard_map(body, mesh=mesh, in_specs=in_specs, out_specs=out_specs, check_vma=False)
```

profile of v0, /device:TPU:1, one launch (start us, length us, event | category | flops | bytes accessed | tf_op | source)
XLA Modules:
  0.0 957.8 jit_solution(635125774649194052)
XLA Ops:
  11.1 24.9 %all-gather.8.cloned.1.call-done = bf16[544,1024]{1,0:T(8,128)(2,1)} async-done(((bf16[136,1024]{1,0:T(8,128)(2,1)}), bf16[544,1024]{1,0:T(8,128)(2,1)}) %all-gather.8.cloned.1.call-update) | async-done | bytes 1114128 | tf_op jit(solution)/shard_map/all_gather | solution.py:50
  40.1 196.5 %all-gather.12.cloned.1.call-done = bf16[1,17408,256]{2,1,0:T(8,128)(2,1)} async-done(((bf16[1,544,256]{2,1,0:T(8,128)(2,1)}), bf16[1,17408,256]{2,1,0:T(8,128)(2,1)}) %all-gather.12.cloned.1.call-update) | async-done | bytes 8912912 | tf_op jit(solution)/shard_map/all_gather | solution.py:67
  236.6 25.9 %reshape.77 = bf16[34,512,4,64]{3,2,1,0:T(4,128)(2,1)} reshape(bf16[1,17408,256]{2,1,0:T(8,128)(2,1)} %all-gather.12.cloned.1.call-done) | data formatting | bytes 17825792 | tf_op jit(solution)/shard_map/reshape | solution.py:70
  262.5 25.6 %copy.24 = bf16[34,512,4,64]{1,3,2,0:T(8,128)(2,1)} copy(bf16[34,512,4,64]{3,2,1,0:T(4,128)(2,1)} %reshape.77) | data formatting | bytes 17825792
  288.2 150.6 %all-gather.14.cloned.1.call-done = bf16[1,17408,256]{2,1,0:T(8,128)(2,1)} async-done(((bf16[1,544,256]{2,1,0:T(8,128)(2,1)}), bf16[1,17408,256]{2,1,0:T(8,128)(2,1)}) %all-gather.14.cloned.1.call-update) | async-done | bytes 8912912 | tf_op jit(solution)/shard_map/all_gather | solution.py:68
  438.8 25.9 %reshape.78 = bf16[34,512,4,64]{3,2,1,0:T(4,128)(2,1)} reshape(bf16[1,17408,256]{2,1,0:T(8,128)(2,1)} %all-gather.14.cloned.1.call-done) | data formatting | bytes 17825792 | tf_op jit(solution)/shard_map/reshape | solution.py:71
  464.7 25.6 %copy.25 = bf16[34,512,4,64]{1,3,2,0:T(8,128)(2,1)} copy(bf16[34,512,4,64]{3,2,1,0:T(4,128)(2,1)} %reshape.78) | data formatting | bytes 17825792
  490.3 298.6 %while.15 = (s32[]{:T(128)}, f32[4,544]{1,0:T(4,128)S(1)}, f32[4,544]{1,0:T(4,128)S(1)}, f32[544,4,64]{0,2,1:T(8,128)S(1)}, bf16[34,512,4,64]{1,3,2,0:T(8,128)(2...) while((s32[]{:T(128)}, f32[4,544]{1,0:T(4,128)S(1)}, ...), condition=%wide.region_4.5_spmd.clone, body=%wide.region_1.4_spmd.clone.sunk | while | flops 294556416 | bytes 33252484 | solution.py:76
  490.3 3.8 bitcast_reduce_fusion.2
  499.2 3.8 bitcast_reduce_fusion.2
  507.9 3.8 bitcast_reduce_fusion.2
  511.7 3.6 fusion.83
  516.7 3.8 bitcast_reduce_fusion.2
  525.5 3.8 bitcast_reduce_fusion.2
  534.3 3.8 bitcast_reduce_fusion.2
  543.1 3.8 bitcast_reduce_fusion.2
  551.9 3.8 bitcast_reduce_fusion.2
  560.6 3.8 bitcast_reduce_fusion.2
  569.4 3.8 bitcast_reduce_fusion.2
  578.2 3.8 bitcast_reduce_fusion.2
  587.0 3.8 bitcast_reduce_fusion.2
  595.8 3.8 bitcast_reduce_fusion.2
  604.5 3.8 bitcast_reduce_fusion.2
  613.3 3.8 bitcast_reduce_fusion.2
  622.1 3.8 bitcast_reduce_fusion.2
  630.9 3.8 bitcast_reduce_fusion.2
  639.7 3.8 bitcast_reduce_fusion.2
  648.4 3.8 bitcast_reduce_fusion.2
  657.2 3.8 bitcast_reduce_fusion.2
  666.0 3.8 bitcast_reduce_fusion.2
  674.8 3.8 bitcast_reduce_fusion.2
  683.6 3.8 bitcast_reduce_fusion.2
  692.4 3.8 bitcast_reduce_fusion.2
  701.1 3.8 bitcast_reduce_fusion.2
  709.9 3.8 bitcast_reduce_fusion.2
  718.7 3.8 bitcast_reduce_fusion.2
  727.5 3.8 bitcast_reduce_fusion.2
  736.3 3.8 bitcast_reduce_fusion.2
  745.0 3.8 bitcast_reduce_fusion.2
  753.8 3.8 bitcast_reduce_fusion.2
  762.6 3.8 bitcast_reduce_fusion.2
  771.4 3.8 bitcast_reduce_fusion.2
  780.2 3.8 bitcast_reduce_fusion.2
  792.4 11.0 %all-gather.2 = bf16[4,2,1024]{2,1,0:T(2,128)(2,1)S(1)} all-gather(bf16[1,2,1024]{2,1,0:T(2,128)(2,1)S(1)} %bitcast.83), channel_id=1, replica_groups=mesh['seq'=32,'type'=4] {'type'}, dimensions={0}, use_global_device_ids=true | all-gather | bytes 20480 | tf_op jit(solution)/shard_map/all_gather | solution.py:103
  803.5 7.4 all_gather.23
  811.0 20.2 %reduce-scatter.2.cloned.1.call-done = f32[136,1024]{1,0:T(8,128)} async-done(((f32[544,1024]{1,0:T(8,128)}), f32[136,1024]{1,0:T(8,128)}) %reduce-scatter.2.cloned.1.call-update) | async-done | bytes 557072 | tf_op jit(solution)/shard_map/reduce_scatter | solution.py:81
  833.3 109.4 %all-gather.10.cloned.1.call-done = bf16[8,1024,1024]{2,1,0:T(8,128)(2,1)} async-done(((bf16[2,1024,1024]{2,1,0:T(8,128)(2,1)}), bf16[8,1024,1024]{2,1,0:T(8,128)(2,1)}) %all-gather.10.cloned.1.call-update) | async-done | bytes 16777232 | tf_op jit(solution)/shard_map/all_gather | solution.py:102
  942.7 7.6 fusion.32
  (297 shorter events, 179.9 us)
Async XLA Ops:
  7.2 28.8 %copy-start = (bf16[3,1024,256]{2,1,0:T(8,128)(2,1)S(1)}, bf16[3,1024,256]{2,1,0:T(8,128)(2,1)}, u32[]{:S(2)}) copy-start(bf16[3,1024,256]{2,1,0:T(8,128)(2,1)} %param.16) | copy-start | bytes 4718596
  7.2 28.7 %all-gather.8.cloned.1.call-start = ((), (), s32[]{:S(2)}) async-start(), calls=%async_computation.1 | async-start | bytes 1392640 | tf_op jit(solution)/shard_map/all_gather | solution.py:50
  11.0 225.6 %all-gather.12.cloned.1.call-start = ((), (), s32[]{:S(2)}) async-start(), calls=%async_computation.4 | async-start | bytes 9191424 | tf_op jit(solution)/shard_map/all_gather | solution.py:67
  39.1 399.7 %all-gather.14.cloned.1.call-start = ((), (), s32[]{:S(2)}) async-start(), calls=%async_computation.5 | async-start | bytes 9191424 | tf_op jit(solution)/shard_map/all_gather | solution.py:68
  39.8 791.4 %reduce-scatter.2.cloned.1.call-start = ((), (), s32[]{:S(2)}) async-start(), calls=%async_computation.2 | async-start | bytes 2785280 | tf_op jit(solution)/shard_map/reduce_scatter | solution.py:81
  490.3 298.7 %copy-start.5 = (bf16[256,1024]{1,0:T(8,128)(2,1)S(1)}, bf16[256,1024]{1,0:T(8,128)(2,1)}, u32[]{:S(2)}) copy-start(bf16[256,1024]{1,0:T(8,128)(2,1)} %param.17) | copy-start | bytes 1572868
  494.2 3.7 copy-start.2
  502.9 3.7 copy-start.2
  511.7 3.7 copy-start.2
  520.5 3.7 copy-start.2
  529.3 3.7 copy-start.2
  538.1 3.7 copy-start.2
  546.8 3.7 copy-start.2
  555.6 3.7 copy-start.2
  564.4 3.7 copy-start.2
  573.2 3.7 copy-start.2
  582.0 3.7 copy-start.2
  590.7 3.7 copy-start.2
  599.5 3.7 copy-start.2
  608.3 3.7 copy-start.2
  617.1 3.7 copy-start.2
  625.9 3.7 copy-start.2
  634.7 3.7 copy-start.2
  643.4 3.7 copy-start.2
  652.2 3.7 copy-start.2
  661.0 3.7 copy-start.2
  669.8 3.7 copy-start.2
  678.6 3.7 copy-start.2
  687.3 3.7 copy-start.2
  696.1 3.7 copy-start.2
  704.9 3.7 copy-start.2
  713.7 3.7 copy-start.2
  722.5 3.7 copy-start.2
  731.3 3.7 copy-start.2
  740.0 3.7 copy-start.2
  748.8 3.7 copy-start.2
  757.6 3.7 copy-start.2
  766.4 3.7 copy-start.2
  775.2 3.7 copy-start.2
  783.9 3.7 copy-start.2
  789.0 3.4 copy-start.10
  789.0 14.4 %copy-start.6 = (bf16[2,1024,16]{1,2,0:T(8,128)(2,1)S(1)}, bf16[2,1024,16]{1,2,0:T(8,128)(2,1)}, u32[]{:S(2)}) copy-start(bf16[2,1024,16]{1,2,0:T(8,128)(2,1)} %param.21) | copy-start | bytes 196612
  789.1 42.2 %copy-start.3 = (bf16[136,1024]{1,0:T(8,128)(2,1)S(1)}, bf16[136,1024]{1,0:T(8,128)(2,1)}, u32[]{:S(2)}) copy-start(bf16[136,1024]{1,0:T(8,128)(2,1)} %param.12) | copy-start | bytes 835588
  789.1 42.2 %copy-start.8 = (f32[1024]{0:T(1024)S(1)}, f32[1024]{0:T(1024)}, u32[]{:S(2)}) copy-start(f32[1024]{0:T(1024)} %param.14) | copy-start | bytes 12292
  790.9 41.6 %copy-start.9 = (f32[1024]{0:T(1024)S(1)}, f32[1024]{0:T(1024)}, u32[]{:S(2)}) copy-start(f32[1024]{0:T(1024)} %param.15) | copy-start | bytes 12292
  791.0 151.7 %all-gather.10.cloned.1.call-start = ((), (), s32[]{:S(2)}) async-start(), calls=%async_computation.3 | async-start | bytes 20971520 | tf_op jit(solution)/shard_map/all_gather | solution.py:102
  832.5 117.8 %copy-start.4 = (bf16[136,1024]{1,0:T(8,128)(2,1)}, bf16[136,1024]{1,0:T(8,128)(2,1)S(1)}, u32[]{:S(2)}) copy-start(bf16[136,1024]{1,0:T(8,128)(2,1)S(1)} %get-tuple-element.104) | copy-start | bytes 835588
  942.7 8.6 copy-start.1
  (1 other events, 2.5 us)
Sparse Core Ops, SparseCore 0:
  11.1 24.7 all-gather.7
  39.2 197.3 all-gather.11
  238.8 199.9 all-gather.13
  791.1 40.1 reduce-scatter.1
  832.8 109.7 all-gather.9
where the time goes:
time: 962 us; the launch traced here: 958 us
  waiting for transfers between devices  503 us (52%)
  matrix products  264 us (27%)
  local copies, waits for them, and re-layouts  106 us (11%)
  other arithmetic  50.4 us (5%)
  blocking collectives  18.4 us (2%)
  between operations  14 us (1%)
    all_gather x1, waiting for transfers between devices, body(): key_part = lax.all_gather(local_keys, 'seq', axis=0, tiled=True)  197 us
    all_gather x1, waiting for transfers between devices, body(): value_part = lax.all_gather(local_values, 'seq', axis=0, tiled=True)  151 us
    dot_general x34, matrix products, absorb_block(): jnp.einsum('qhd,khd->hqk', query_heads, key_heads, preferred_element_type...  128 us
    dot_general x34, matrix products, absorb_block(): jnp.einsum('hqk,khd->qhd', weights.astype(jnp.bfloat16), value_heads, pre...  123 us
    all_gather x1, waiting for transfers between devices, body(): lax.all_gather(head_w1, 'type', axis=0, tiled=True)  109 us
    unnamed x22, local copies, waits for them, and re-layouts  51.3 us
    reduce_sum x34, other arithmetic, absorb_block(): totals = totals * decay + jnp.sum(weights, axis=-1)  43.5 us
    reshape x1, local copies, waits for them, and re-layouts, body(): key_blocks = key_part.reshape(row_total // 512, 512, local_heads, HD)  25.9 us
  transfers between devices with their start and end apart: 5, of which 5 were waited for; matrix products, arithmetic and copies ran while one was open for 6% of the time, Pallas kernels for 0%

commit v1 on v0

--- a/solution.py
+++ b/solution.py
@@ -64,8 +64,13 @@
         jnp.zeros((query_count, local_heads, HD), jnp.float32),
     )
     running = initial
-    key_part = lax.all_gather(local_keys, "seq", axis=0, tiled=True)
-    value_part = lax.all_gather(local_values, "seq", axis=0, tiled=True)
+    key_part, value_part = jnp.split(
+        lax.all_gather(
+            jnp.concatenate([local_keys, local_values], axis=1), "seq", axis=0, tiled=True
+        ),
+        [local_keys.shape[1]],
+        axis=1,
+    )
     row_total = key_part.shape[0]
     key_blocks = key_part.reshape(row_total // 512, 512, local_heads, HD)
     value_blocks = value_part.reshape(row_total // 512, 512, local_heads, HD)

time: 962 us -> 1010 us (1.050)
  waiting for transfers between devices: 503 us -> 540 us
  local copies, waits for them, and re-layouts: 106 us -> 117 us
    all_gather x2 -> x1, waiting for transfers between devices: 347 us -> 383 us  [body(): lax.all_gather(jnp.concatenate([local_keys, local_values], axis=1), 'seq'...]
    split x0 -> x1, local copies, waits for them, and re-layouts: none -> 12 us  [body(): jnp.split(lax.all_gather(jnp.concatenate([local_keys, local_values], axis...]
  transfers between devices with their start and end apart: 5 -> 4, of which waited for: 5 -> 4; matrix products, arithmetic and copies ran while one was open for 6% -> 0% of each run, Pallas kernels for 0% -> 0%
where the time goes in v1:
time: 1010 us; the launch traced here: 1000 us
  waiting for transfers between devices  540 us (53%)
  matrix products  265 us (26%)
  local copies, waits for them, and re-layouts  117 us (12%)
  other arithmetic  51.2 us (5%)
  blocking collectives  14.7 us (1%)
  between operations  14 us (1%)
    all_gather x1, waiting for transfers between devices, body(): lax.all_gather(jnp.concatenate([local_keys, local_values], axis=1), 'seq'...  383 us
    dot_general x34, matrix products, absorb_block(): jnp.einsum('qhd,khd->hqk', query_heads, key_heads, preferred_element_type...  129 us
    dot_general x34, matrix products, absorb_block(): jnp.einsum('hqk,khd->qhd', weights.astype(jnp.bfloat16), value_heads, pre...  123 us
    all_gather x1, waiting for transfers between devices, body(): lax.all_gather(head_w1, 'type', axis=0, tiled=True)  109 us
    unnamed x22, local copies, waits for them, and re-layouts  51.3 us
    reduce_sum x34, other arithmetic, absorb_block(): totals = totals * decay + jnp.sum(weights, axis=-1)  43.5 us
    reshape x1, local copies, waits for them, and re-layouts, body(): key_blocks = key_part.reshape(row_total // 512, 512, local_heads, HD)  25.9 us
    reshape x1, local copies, waits for them, and re-layouts, body(): value_blocks = value_part.reshape(row_total // 512, 512, local_heads, HD)  25.9 us
  transfers between devices with their start and end apart: 4, of which 4 were waited for; matrix products, arithmetic and copies ran while one was open for 0% of the time, Pallas kernels for 0%

profile of v1, /device:TPU:1, one launch (start us, length us, event | category | flops | bytes accessed | tf_op | source)
XLA Modules:
  0.0 1003.3 jit_solution(5186947992666180060)
XLA Ops:
  11.1 24.9 %all-gather.5.cloned.1.call-done = bf16[544,1024]{1,0:T(8,128)(2,1)} async-done(((bf16[136,1024]{1,0:T(8,128)(2,1)}), bf16[544,1024]{1,0:T(8,128)(2,1)}) %all-gather.5.cloned.1.call-update) | async-done | bytes 1114128 | tf_op jit(solution)/shard_map/all_gather | solution.py:50
  39.4 382.9 %all-gather.7.cloned.1.call-done = bf16[17408,512]{1,0:T(8,128)(2,1)} async-done(((bf16[544,512]{1,0:T(8,128)(2,1)}), bf16[17408,512]{1,0:T(8,128)(2,1)}) %all-gather.7.cloned.1.call-update) | async-done | bytes 17825808 | tf_op jit(solution)/shard_map/all_gather | solution.py:68
  422.3 12.0 %fusion.60 = (bf16[17408,256]{1,0:T(8,128)(2,1)}, bf16[17408,256]{1,0:T(8,128)(2,1)}) fusion(bf16[17408,512]{1,0:T(8,128)(2,1)} %all-gather.7.cloned.1.call-done), kind=kLoop, calls=%fused_computation.84 | loop fusion | bytes 35651584 | tf_op jit(solution)/shard_map/split | solution.py:67
  434.3 25.9 %reshape.73 = bf16[34,512,4,64]{3,2,1,0:T(4,128)(2,1)} reshape(bf16[17408,256]{1,0:T(8,128)(2,1)} %get-tuple-element.108) | data formatting | bytes 17825792 | tf_op jit(solution)/shard_map/reshape | solution.py:75
  460.2 25.6 %copy.24 = bf16[34,512,4,64]{1,3,2,0:T(8,128)(2,1)} copy(bf16[34,512,4,64]{3,2,1,0:T(4,128)(2,1)} %reshape.73) | data formatting | bytes 17825792
  485.8 25.9 %reshape.74 = bf16[34,512,4,64]{3,2,1,0:T(4,128)(2,1)} reshape(bf16[17408,256]{1,0:T(8,128)(2,1)} %get-tuple-element.107) | data formatting | bytes 17825792 | tf_op jit(solution)/shard_map/reshape | solution.py:76
  511.7 25.6 %copy.25 = bf16[34,512,4,64]{1,3,2,0:T(8,128)(2,1)} copy(bf16[34,512,4,64]{3,2,1,0:T(4,128)(2,1)} %reshape.74) | data formatting | bytes 17825792
  537.3 299.0 %while.15 = (s32[]{:T(128)}, f32[4,544]{1,0:T(4,128)S(1)}, f32[4,544]{1,0:T(4,128)S(1)}, f32[544,4,64]{0,2,1:T(8,128)S(1)}, bf16[34,512,4,64]{1,3,2,0:T(8,128)(2...) while((s32[]{:T(128)}, f32[4,544]{1,0:T(4,128)S(1)}, ...), condition=%wide.region_4.5_spmd.clone, body=%wide.region_1.4_spmd.clone.sunk | while | flops 294556416 | bytes 33252484 | solution.py:81
  537.3 3.8 bitcast_reduce_fusion.2
  541.2 3.6 fusion.84
  546.2 3.8 bitcast_reduce_fusion.2
  555.0 3.8 bitcast_reduce_fusion.2
  563.8 3.8 bitcast_reduce_fusion.2
  572.5 3.8 bitcast_reduce_fusion.2
  581.3 3.8 bitcast_reduce_fusion.2
  590.1 3.8 bitcast_reduce_fusion.2
  598.9 3.8 bitcast_reduce_fusion.2
  607.7 3.8 bitcast_reduce_fusion.2
  616.5 3.8 bitcast_reduce_fusion.2
  625.3 3.8 bitcast_reduce_fusion.2
  634.1 3.8 bitcast_reduce_fusion.2
  642.9 3.8 bitcast_reduce_fusion.2
  651.7 3.8 bitcast_reduce_fusion.2
  660.5 3.8 bitcast_reduce_fusion.2
  669.3 3.8 bitcast_reduce_fusion.2
  678.0 3.8 bitcast_reduce_fusion.2
  686.8 3.8 bitcast_reduce_fusion.2
  695.6 3.8 bitcast_reduce_fusion.2
  704.4 3.8 bitcast_reduce_fusion.2
  713.2 3.8 bitcast_reduce_fusion.2
  722.0 3.8 bitcast_reduce_fusion.2
  730.8 3.8 bitcast_reduce_fusion.2
  739.6 3.8 bitcast_reduce_fusion.2
  748.4 3.8 bitcast_reduce_fusion.2
  757.2 3.8 bitcast_reduce_fusion.2
  766.0 3.8 bitcast_reduce_fusion.2
  774.8 3.8 bitcast_reduce_fusion.2
  783.5 3.8 bitcast_reduce_fusion.2
  792.3 3.8 bitcast_reduce_fusion.2
  801.1 3.8 bitcast_reduce_fusion.2
  809.9 3.8 bitcast_reduce_fusion.2
  818.7 3.8 bitcast_reduce_fusion.2
  827.5 3.8 bitcast_reduce_fusion.2
  839.8 7.3 all-gather
  847.1 7.4 all_gather.19
  854.6 22.1 %reduce-scatter.2.cloned.1.call-done = f32[136,1024]{1,0:T(8,128)} async-done(((f32[544,1024]{1,0:T(8,128)}), f32[136,1024]{1,0:T(8,128)}) %reduce-scatter.2.cloned.1.call-update) | async-done | bytes 557072 | tf_op jit(solution)/shard_map/reduce_scatter | solution.py:86
  878.7 109.4 %all-gather.9.cloned.1.call-done = bf16[8,1024,1024]{2,1,0:T(8,128)(2,1)} async-done(((bf16[2,1024,1024]{2,1,0:T(8,128)(2,1)}), bf16[8,1024,1024]{2,1,0:T(8,128)(2,1)}) %all-gather.9.cloned.1.call-update) | async-done | bytes 16777232 | tf_op jit(solution)/shard_map/all_gather | solution.py:107
  988.2 7.6 fusion.32
  (296 shorter events, 179.3 us)
Async XLA Ops:
  7.2 28.8 %copy-start = (bf16[3,1024,256]{2,1,0:T(8,128)(2,1)S(1)}, bf16[3,1024,256]{2,1,0:T(8,128)(2,1)}, u32[]{:S(2)}) copy-start(bf16[3,1024,256]{2,1,0:T(8,128)(2,1)} %param.16) | copy-start | bytes 4718596
  7.2 28.7 %all-gather.5.cloned.1.call-start = ((), (), s32[]{:S(2)}) async-start(), calls=%async_computation.1 | async-start | bytes 1392640 | tf_op jit(solution)/shard_map/all_gather | solution.py:50
  11.0 411.3 %all-gather.7.cloned.1.call-start = ((), (), s32[]{:S(2)}) async-start(), calls=%async_computation.2 | async-start | bytes 18382848 | tf_op jit(solution)/shard_map/all_gather | solution.py:68
  39.2 837.5 %reduce-scatter.2.cloned.1.call-start = ((), (), s32[]{:S(2)}) async-start(), calls=%async_computation.3 | async-start | bytes 2785280 | tf_op jit(solution)/shard_map/reduce_scatter | solution.py:86
  537.3 299.0 %copy-start.5 = (bf16[256,1024]{1,0:T(8,128)(2,1)S(1)}, bf16[256,1024]{1,0:T(8,128)(2,1)}, u32[]{:S(2)}) copy-start(bf16[256,1024]{1,0:T(8,128)(2,1)} %param.17) | copy-start | bytes 1572868
  541.2 3.7 copy-start.2
  550.0 3.7 copy-start.2
  558.7 3.7 copy-start.2
  567.5 3.7 copy-start.2
  576.3 3.7 copy-start.2
  585.1 3.7 copy-start.2
  593.9 3.7 copy-start.2
  602.7 3.7 copy-start.2
  611.5 3.7 copy-start.2
  620.3 3.7 copy-start.2
  629.1 3.7 copy-start.2
  637.9 3.7 copy-start.2
  646.7 3.7 copy-start.2
  655.5 3.7 copy-start.2
  664.2 3.7 copy-start.2
  673.0 3.7 copy-start.2
  681.8 3.7 copy-start.2
  690.6 3.7 copy-start.2
  699.4 3.7 copy-start.2
  708.2 3.7 copy-start.2
  717.0 3.7 copy-start.2
  725.8 3.7 copy-start.2
  734.6 3.7 copy-start.2
  743.4 3.7 copy-start.2
  752.2 3.7 copy-start.2
  761.0 3.7 copy-start.2
  769.7 3.7 copy-start.2
  778.5 3.7 copy-start.2
  787.3 3.7 copy-start.2
  796.1 3.7 copy-start.2
  804.9 3.7 copy-start.2
  813.7 3.7 copy-start.2
  822.5 3.7 copy-start.2
  831.3 3.7 copy-start.2
  836.4 2.5 copy-start.7
  836.4 3.4 copy-start.10
  836.4 10.7 %copy-start.6 = (bf16[2,1024,16]{1,2,0:T(8,128)(2,1)S(1)}, bf16[2,1024,16]{1,2,0:T(8,128)(2,1)}, u32[]{:S(2)}) copy-start(bf16[2,1024,16]{1,2,0:T(8,128)(2,1)} %param.21) | copy-start | bytes 196612
  836.4 40.3 %copy-start.3 = (bf16[136,1024]{1,0:T(8,128)(2,1)S(1)}, bf16[136,1024]{1,0:T(8,128)(2,1)}, u32[]{:S(2)}) copy-start(bf16[136,1024]{1,0:T(8,128)(2,1)} %param.12) | copy-start | bytes 835588
  836.4 40.3 %copy-start.8 = (f32[1024]{0:T(1024)S(1)}, f32[1024]{0:T(1024)}, u32[]{:S(2)}) copy-start(f32[1024]{0:T(1024)} %param.14) | copy-start | bytes 12292
  838.3 39.7 %copy-start.9 = (f32[1024]{0:T(1024)S(1)}, f32[1024]{0:T(1024)}, u32[]{:S(2)}) copy-start(f32[1024]{0:T(1024)} %param.15) | copy-start | bytes 12292
  838.3 149.9 %all-gather.9.cloned.1.call-start = ((), (), s32[]{:S(2)}) async-start(), calls=%async_computation.4 | async-start | bytes 20971520 | tf_op jit(solution)/shard_map/all_gather | solution.py:107
  877.9 117.8 %copy-start.4 = (bf16[136,1024]{1,0:T(8,128)(2,1)}, bf16[136,1024]{1,0:T(8,128)(2,1)S(1)}, u32[]{:S(2)}) copy-start(bf16[136,1024]{1,0:T(8,128)(2,1)S(1)} %get-tuple-element.104) | copy-start | bytes 835588
  988.2 8.6 copy-start.1
Sparse Core Ops, SparseCore 0:
  11.1 24.7 all-gather.4
  39.3 382.9 all-gather.6
  838.4 38.2 reduce-scatter.1
  878.3 109.7 all-gather.8
